TPU v7x, 32 devices: a whole 2x2x4 slice. The times are simulated.
32 devices in a mesh: group: 2 (over y), seq: 8 (over z, x), chan: 2 (over core).
Axes of the slice: x: 2, y: 2, z: 4, core: 2. Of those that a mesh axis runs over, the one named last changes fastest.
Arguments:
- fresh: bfloat16 [2048, 3, 2048], P(('group', 'seq'), None, 'chan'), parts along dimension 0, may hold values from -6 to 6
- library: bfloat16 [8, 8, 2048], P('seq', None, 'chan'), may hold values from -6 to 6
- block_slot: int32 [8], replicated, may hold values from 0 to 7, each once
- prefix_blocks: int32 [16, 4], P('group'), parts along dimension 0, may hold values from 0 to 7, all different within a row
- short_taps: float32 [3, 3, 2048], P(None, None, 'chan'), may hold values from -4 to 4
- long_filter: float32 [1024, 2048], P('seq', 'chan'), may hold values from -2 to 2
- skip_gain: float32 [2048], P('chan'), may hold values from -6 to 6
Outputs:
- mixed: bfloat16 [2048, 2048], P(('group', 'seq'), 'chan'), parts along dimension 0
There are 2 independent parts, one for each index of `group`. A program takes and returns all parts, laid end to end along the dimension named above; an argument that names none is the same for every part. Nothing has to cross between parts.
Inputs may be any that keep to these rules, and one draw needn't show every extreme that they name: `block_slot`: each number appears once. `prefix_blocks`: every library block is named at least once; the four entries of a row differ.
All inputs are finite; a program needn't handle non-finite values.
Results may differ from a plain program's by a relative error of at most 0.008.
Values may be sent and summed in bfloat16 or wider, within the bound.
No kernel may reach another device: no remote copies, remote signals or barrier semaphores. Data moves between devices by JAX's collectives and lax.ppermute only.
A program may use at most 64 MiB of HBM per device.

v0:
```python
import math
import jax
import jax.numpy as jnp
from jax import lax
from jax.sharding import PartitionSpec as P

TAPS = 3
BLK = 8


def from_behind(shard, axis, by):
    count = lax.axis_size(axis)
    pairs = [(i, i + by) for i in range(count) if 0 <= i + by < count]
    return lax.ppermute(shard, axis, pairs)


def exact_dot(pattern, matrix, tensor):
    return jnp.einsum(pattern, matrix, tensor, precision=lax.Precision.HIGHEST)


def turn_angles(numbers, period):
    return (numbers % period).astype(jnp.float32) * (2.0 * math.pi / period)


def ring_body(fresh, library, block_slot, prefix_blocks, short_taps, long_filter, skip_gain):
    row_count = fresh.shape[0]
    channels = fresh.shape[2]
    devices = lax.axis_size("seq")
    seq_index = lax.axis_index("seq")
    group_rows = row_count // devices
    period = 2 * row_count * devices
    block_ids = jnp.arange(devices, dtype=jnp.int32)
    mode_ids = jnp.arange(2 * devices, dtype=jnp.int32)
    coarse = turn_angles(mode_ids[:, None] * block_ids[None, :], 2 * devices)
    cos_q = jnp.cos(coarse)
    sin_q = jnp.sin(coarse)
    local_rows = seq_index * group_rows + jnp.arange(group_rows, dtype=jnp.int32)
    twist = turn_angles(mode_ids[:, None] * local_rows[None, :], period)
    twist_cos = jnp.cos(twist)[:, :, None]
    twist_sin = jnp.sin(twist)[:, :, None]
    row_ids = jnp.arange(row_count, dtype=jnp.int32)
    fine_angles = turn_angles(row_ids[:, None] * row_ids[None, :], row_count)
    cos_m = jnp.cos(fine_angles)
    sin_m = jnp.sin(fine_angles)
    first_modes = 2 * seq_index + jnp.arange(2, dtype=jnp.int32)
    back_twist = turn_angles(first_modes[:, None] * row_ids[None, :], period)
    back_cos = jnp.cos(back_twist)[:, :, None]
    back_sin = jnp.sin(back_twist)[:, :, None]

    def to_modes(column):
        real_part = exact_dot("kq,qgc->kgc", cos_q, column)
        imag_part = -exact_dot("kq,qgc->kgc", sin_q, column)
        return jnp.stack(
            [
                real_part * twist_cos + imag_part * twist_sin,
                imag_part * twist_cos - real_part * twist_sin,
            ]
        )

    def to_spectrum(spread):
        real_part = exact_dot("ki,jic->jkc", cos_m, spread[0]) + exact_dot(
            "ki,jic->jkc", sin_m, spread[1]
        )
        imag_part = exact_dot("ki,jic->jkc", cos_m, spread[1]) - exact_dot(
            "ki,jic->jkc", sin_m, spread[0]
        )
        return (real_part, imag_part)

    blocks_here = row_count // BLK
    flat_ids = prefix_blocks.reshape(-1)
    first_block = jnp.minimum(seq_index * blocks_here, flat_ids.shape[0] - blocks_here)
    own_ids = lax.dynamic_slice_in_dim(flat_ids, first_block, blocks_here)
    matches = own_ids[:, None] == jnp.arange(block_slot.shape[0], dtype=jnp.int32)[None, :]
    wanted = jnp.sum(jnp.where(matches, block_slot[None, :], 0), axis=1)
    shards = lax.all_gather(library, "seq", axis=0, tiled=True)
    picker = (wanted[:, None] == jnp.arange(shards.shape[0], dtype=jnp.int32)[None, :]).astype(
        jnp.bfloat16
    )
    gathered = jnp.einsum("bn,nlc->blc", picker, shards, preferred_element_type=jnp.float32)
    cached = gathered.reshape(row_count, channels).astype(jnp.bfloat16)
    values = jnp.where(seq_index < devices // 4, cached, fresh[:, 2])
    stacked = jnp.concatenate([fresh[:, :2], values[:, None]], axis=1)
    previous = from_behind(stacked[row_count - (TAPS - 1) :], "seq", 1)
    extended = jnp.concatenate([previous, stacked], axis=0)
    shortened = jnp.zeros((row_count, 3, channels), jnp.float32)
    for offset in range(TAPS):
        window_start = TAPS - 1 - offset
        shortened = shortened + short_taps[offset][None] * extended[
            window_start : window_start + row_count
        ].astype(jnp.float32)
    gating = shortened[:, 0]
    signal = shortened[:, 1] * shortened[:, 2]
    spread_signal = to_modes(
        lax.all_to_all(signal[None], "seq", split_axis=1, concat_axis=0, tiled=True)
    )
    spread_taps = to_modes(
        lax.all_to_all(long_filter[None], "seq", split_axis=1, concat_axis=0, tiled=True)
    )
    moved_signal, moved_taps = (
        lax.all_to_all(
            spread_signal.astype(jnp.bfloat16), "seq", split_axis=1, concat_axis=2, tiled=True
        ).astype(spread_signal.dtype),
        lax.all_to_all(
            spread_taps.astype(jnp.bfloat16), "seq", split_axis=1, concat_axis=2, tiled=True
        ).astype(spread_taps.dtype),
    )
    sig_real, sig_imag = to_spectrum(moved_signal)
    tap_real, tap_imag = to_spectrum(moved_taps)
    prod_real = sig_real * tap_real - sig_imag * tap_imag
    prod_imag = sig_real * tap_imag + sig_imag * tap_real
    back_real = exact_dot("ki,jic->jkc", cos_m, prod_real) - exact_dot(
        "ki,jic->jkc", sin_m, prod_imag
    )
    back_imag = exact_dot("ki,jic->jkc", cos_m, prod_imag) + exact_dot(
        "ki,jic->jkc", sin_m, prod_real
    )
    turned = jnp.stack(
        [back_real * back_cos - back_imag * back_sin, back_imag * back_cos + back_real * back_sin]
    )
    spread = lax.all_to_all(turned, "seq", split_axis=2, concat_axis=1, tiled=True)
    positions = (
        exact_dot("kq,kgc->qgc", cos_q, spread[0]) - exact_dot("kq,kgc->qgc", sin_q, spread[1])
    ) / period
    convolved = lax.all_to_all(positions, "seq", split_axis=0, concat_axis=1, tiled=True)[0]
    output = gating * (convolved + skip_gain[None, :] * signal)
    return output.astype(jnp.bfloat16)


def dft_tables(tokens):
    period = 2 * tokens
    width = 1
    while width * width < tokens:
        width *= 2
    outer = tokens // width
    freqs = jnp.arange(tokens + 1, dtype=jnp.int32)[:, None]
    coarse = turn_angles(freqs * (width * jnp.arange(outer, dtype=jnp.int32))[None, :], period)
    fine = turn_angles(freqs * jnp.arange(width, dtype=jnp.int32)[None, :], period)
    c1, s1 = (jnp.cos(coarse)[:, :, None], jnp.sin(coarse)[:, :, None])
    c2, s2 = (jnp.cos(fine)[:, None, :], jnp.sin(fine)[:, None, :])
    cos_t = (c1 * c2 - s1 * s2).reshape(tokens + 1, tokens)
    sin_t = (s1 * c2 + c1 * s2).reshape(tokens + 1, tokens)
    return (cos_t, sin_t)


def local_body(fresh, library, block_slot, prefix_blocks, short_taps, long_filter, skip_gain):
    row_count, _, channels = fresh.shape
    devices = lax.axis_size("seq")
    seq_index = lax.axis_index("seq")
    tokens = row_count * devices
    own = channels // devices
    lib_here = library.shape[0]
    lib_rows = lib_here * BLK // 4
    packed = jnp.concatenate([fresh, long_filter.astype(jnp.bfloat16)[:, None, :]], axis=1)
    packed = jnp.concatenate([packed, library.reshape(lib_rows, 4, channels)], axis=0)
    packed = packed.reshape(row_count + lib_rows, 4, devices, own).transpose(2, 0, 1, 3)
    moved = lax.all_to_all(packed, "seq", split_axis=0, concat_axis=0, tiled=True)
    rows = moved[:, :row_count].reshape(tokens, 4, own)
    lib_all = moved[:, row_count:].reshape(devices * lib_here, BLK * own)
    slot_ids = block_slot[prefix_blocks.reshape(-1)]
    prefix_len = slot_ids.shape[0] * BLK
    picker = (slot_ids[:, None] == jnp.arange(lib_all.shape[0], dtype=jnp.int32)[None, :]).astype(
        jnp.bfloat16
    )
    cached = jnp.dot(picker, lib_all, preferred_element_type=jnp.float32)
    cached = cached.reshape(prefix_len, own).astype(jnp.bfloat16)
    values = jnp.concatenate([cached, rows[prefix_len:, 2]], axis=0)
    stacked = jnp.concatenate([rows[:, :2], values[:, None]], axis=1).astype(jnp.float32)
    taps = lax.dynamic_slice_in_dim(short_taps, seq_index * own, own, axis=2)
    gain = lax.dynamic_slice_in_dim(skip_gain, seq_index * own, own, axis=0)
    shortened = jnp.zeros((tokens, 3, own), jnp.float32)
    for offset in range(TAPS):
        shifted = jnp.pad(stacked[: tokens - offset], ((offset, 0), (0, 0), (0, 0)))
        shortened = shortened + taps[offset][None] * shifted
    gating = shortened[:, 0]
    signal = shortened[:, 1] * shortened[:, 2]
    cos_t, sin_t = dft_tables(tokens)
    table = jnp.concatenate([cos_t, sin_t], axis=0).astype(jnp.bfloat16)
    operands = jnp.concatenate([signal.astype(jnp.bfloat16), rows[:, 3]], axis=1)
    spec = jnp.dot(table, operands, preferred_element_type=jnp.float32)
    bins = tokens + 1
    sig_c, tap_c = (spec[:bins, :own], spec[:bins, own:])
    sig_s, tap_s = (spec[bins:, :own], spec[bins:, own:])
    weight = jnp.where((jnp.arange(bins) == 0) | (jnp.arange(bins) == tokens), 1.0, 2.0).astype(
        jnp.float32
    )[:, None] / (2 * tokens)
    real = (sig_c * tap_c - sig_s * tap_s) * weight
    turned = (sig_c * tap_s + sig_s * tap_c) * weight
    back = jnp.concatenate([real, turned], axis=0).astype(jnp.bfloat16)
    convolved = lax.dot_general(
        table, back, (((0,), (0,)), ((), ())), preferred_element_type=jnp.float32
    )
    output = (gating * (convolved + gain[None, :] * signal)).astype(jnp.bfloat16)
    output = lax.all_to_all(
        output.reshape(devices, row_count, own), "seq", split_axis=0, concat_axis=0, tiled=True
    )
    return output.transpose(1, 0, 2).reshape(row_count, channels)


def body(fresh, library, *rest):
    devices = lax.axis_size("seq")
    tokens = fresh.shape[0] * devices
    fits = tokens <= 4096 and fresh.shape[2] % devices == 0 and (library.shape[0] * BLK % 4 == 0)
    if fits:
        return local_body(fresh, library, *rest)
    return ring_body(fresh, library, *rest)


def solution(mesh):
    return jax.shard_map(
        body,
        mesh=mesh,
        in_specs=(
            P(("group", "seq"), None, "chan"),
            P("seq", None, "chan"),
            P(),
            P("group", None),
            P(None, None, "chan"),
            P("seq", "chan"),
            P("chan"),
        ),
        out_specs=P(("group", "seq"), "chan"),
        check_vma=False,
    )
```

profile of v0, /device:TPU:0, one launch (start us, length us, event | category | flops | bytes accessed | tf_op | source)
XLA Modules:
  0.0 62.9 jit_solution(6470833181533852721)
XLA Ops:
  0.0 0.0 copy-start
  0.0 0.7 %copy.40 = bf16[1,8,8,128]{3,2,1,0:T(8,128)(2,1)S(1)} copy(bf16[1,8,8,128]{3,1,2,0:T(8,128)(2,1)} %bitcast.60) | data formatting | bytes 32768
  0.7 1.1 %convert_element_type.49 = bf16[128,1024]{1,0:T(8,128)(2,1)S(1)} convert(f32[128,1024]{1,0:T(8,128)} %param.12) | non-fusion elementwise | flops 131072 | bytes 786432 | tf_op jit(solution)/shard_map/convert_element_type | solution.py:153
  1.8 0.2 copy.31
  2.0 2.3 %copy.30 = bf16[128,3,1024]{0,2,1:T(8,128)(2,1)} copy(bf16[128,3,1024]{2,0,1:T(8,128)(2,1)} %param.7) | data formatting | bytes 1572864 | tf_op args[0]
  4.3 0.5 copy.32
  4.8 1.7 %maximum_bitcast_fusion = bf16[8,130,4,128]{1,3,0,2:T(8,128)(2,1)S(1)} fusion(bf16[2,4,8,128]{0,3,2,1:T(8,128)(2,1)S(1)} %copy.32, bf16[128,1,8,128]{0,3,2,1:T(8,128)(2,1)S(1)} %bitcast.56, bf16[128,3,8,128]{0,3,2,1:T(8,128)(2,1)} %bitcast.51), kind=kLoop, calls=%fused_computation.6 | loop fusion | flops 3194880 | bytes 2129920 | tf_op jit(solution)/shard_map/transpose | solution.py:155
  6.5 0.0 copy-start.3
  6.5 2.3 %copy.33 = bf16[8,130,4,128]{3,2,1,0:T(4,128)(2,1)} copy(bf16[8,130,4,128]{1,3,0,2:T(8,128)(2,1)S(1)} %maximum_bitcast_fusion) | data formatting | bytes 2129920 | tf_op jit(solution)/shard_map/transpose | solution.py:155
  8.8 7.3 %all-to-all-start = ((bf16[8,130,4,128]{3,2,1,0:T(4,128)(2,1)}), bf16[8,130,4,128]{3,2,1,0:T(4,128)(2,1)S(1)}, u32[]{:S(2)}, u32[]{:S(2)}) async-start(bf16[8,130,4,128]{3,2,1,0:T(4,128)(2,1)} %copy.33), calls=%async_computation | async-start | bytes 2129920 | tf_op jit(solution)/shard_map/all_to_all | solution.py:156
  16.1 0.1 copy.35
  16.2 0.1 reshape.176
  16.3 0.8 %dynamic_slice.7 = f32[128]{0:T(128)S(1)} dynamic-slice(f32[1024]{0:T(1024)} %param.13, s32[]{:T(128)S(6)} %select_n.53), dynamic_slice_sizes={128} | dynamic-slice | bytes 1028 | tf_op jit(solution)/shard_map/dynamic_slice | solution.py:169
  17.1 0.7 %gather_fusion = s32[32]{0:T(128)S(1)} fusion(s32[8]{0:T(128)S(1)} %copy-done, s32[1024]{0:T(1024)S(1)} %pad_clamp_fusion), kind=kCustom, calls=%fused_computation | custom fusion | bytes 384 | tf_op jit(solution)/shard_map/gather | solution.py:159
  17.8 0.7 %dynamic-slice_bitcast_fusion.2 = (f32[3,128]{1,0:T(4,128)S(1)}, f32[3,128]{1,0:T(4,128)S(1)}, f32[3,128]{1,0:T(4,128)S(1)}) fusion(f32[3,3,1024]{2,1,0:T(4,128)} %param.11, s32[]{:T(128)S(6)} %select_n.53, s32[]{:T(128)S(6)} %add.79, s32[]{:T(128)S(6)} %add.80), kind=kLoop, calls=%fused_computation.61 | loop fusion | bytes 9228 | tf_op jit(solution)/shard_map/mul | solution.py:173
  18.5 0.6 fusion.25
  19.1 0.7 %fusion.28 = (f32[1025,32]{0,1:T(8,128)S(1)}, f32[1025,32]{0,1:T(8,128)S(1)}) fusion(s32[32]{0:T(128)S(1)} %iota_multiply_fusion), kind=kLoop, calls=%fused_computation.50 | loop fusion | flops 459200 | bytes 262528 | tf_op jit(solution)/shard_map/cos | solution.py:138
  19.7 3.7 %subtract_convert_fusion = (bf16[1025,32,32]{0,2,1:T(8,128)(2,1)}, bf16[1025,32,32]{0,2,1:T(8,128)(2,1)}) fusion(f32[1025,32]{0,1:T(8,128)S(1)} %get-tuple-element.14, f32[1025,32]{0,1:T(8,128)S(1)} %get-tuple-element.13, f32[1025,32]{0,1:T(8,128)S(1)} %get-tuple-element.15, f32[1025,32]{0,1:T(8,128)S(1)} %get-tuple-element.12), kind=kLoop, calls=%fused_computation.2 | loop fusion | flops 8396800 | bytes 4723200 | tf_op jit(solution)/shard_map/convert.5
  23.4 18.8 %all-to-all-done = bf16[8,130,4,128]{3,2,1,0:T(4,128)(2,1)S(1)} async-done(((bf16[8,130,4,128]{3,2,1,0:T(4,128)(2,1)}), bf16[8,130,4,128]{3,2,1,0:T(4,128)(2,1)S(1)}, u32[]{:S(2)}, u32[]{:S(2)}) %all-to-all-start) | async-done | bytes 1064992 | tf_op jit(solution)/shard_map/all_to_all | solution.py:156
  42.2 0.4 slice.70
  42.6 0.2 copy.34
  42.9 0.2 convolution_convert_fusion
  43.2 0.1 maximum_convert_fusion
  43.4 0.5 multiply_add_fusion
  43.9 0.1 fusion.12
  44.0 1.0 %copy-done.1 = bf16[1025,32,32]{0,2,1:T(8,128)(2,1)S(1)} copy-done((bf16[1025,32,32]{0,2,1:T(8,128)(2,1)S(1)}, bf16[1025,32,32]{0,2,1:T(8,128)(2,1)}, u32[]{:S(2)}) %copy-start.1) | copy-done | bytes 2099224
  45.0 0.7 %copy-done.2 = bf16[1025,32,32]{0,2,1:T(8,128)(2,1)S(1)} copy-done((bf16[1025,32,32]{0,2,1:T(8,128)(2,1)S(1)}, bf16[1025,32,32]{0,2,1:T(8,128)(2,1)}, u32[]{:S(2)}) %copy-start.2) | copy-done | bytes 2099224
  45.7 2.2 %fusion.1 = f32[2050,256]{1,0:T(8,128)S(1)} fusion(bf16[1025,1024]{0,1:T(8,128)(2,1)S(1)} %bitcast.54, bf16[1025,1024]{0,1:T(8,128)(2,1)S(1)} %bitcast.52, bf16[1024,128]{1,0:T(8,128)(2,1)S(1)} %slice_bitcast_fusion.1, bf16[1024,128]{1,0:T(8,128)(2,1)S(1)} %fusion.12), kind=kOutput, calls=%fused_computation.5 | convolution fusion | flops 1084235776 | bytes 6821888 | tf_op jit(solution)/shard_map/dot_general | solution.py:179
  47.9 0.3 multiply_convert_fusion.1
  48.2 1.4 %fusion.4 = bf16[1024,128]{1,0:T(8,128)(2,1)S(1)} fusion(bf16[1025,1024]{0,1:T(8,128)(2,1)S(1)} %bitcast.55, bf16[1025,1024]{0,1:T(8,128)(2,1)S(1)} %bitcast.53, bf16[1025,128]{1,0:T(8,128)(2,1)S(1)} %get-tuple-element.6, bf16[1025,128]{1,0:T(8,128)(2,1)S(1)} %get-tuple-element.5, f32[1024,3,128]{2,0,1:T(8,128)S(1)} %multiply_add_fusion, ...), kind=kOutput, calls=%fused_computation.10 | convolution fusion | flops 547496960 | bytes 6558720 | tf_op jit(solution)/shard_map/dot_general | solution.py:189
  49.6 12.5 %all_to_all.10 = bf16[8,128,128]{2,1,0:T(8,128)(2,1)S(1)} all-to-all(bf16[8,128,128]{2,1,0:T(8,128)(2,1)S(1)} %bitcast.57), channel_id=1, replica_groups=mesh['group'=2,'seq'=8,'chan'=2] {'seq'}, dimensions={0} | all-to-all | bytes 524288 | tf_op jit(solution)/shard_map/all_to_all | solution.py:193
  62.1 0.7 %copy_bitcast_fusion = bf16[128,1024]{1,0:T(8,128)(2,1)} fusion(bf16[8,128,128]{2,1,0:T(8,128)(2,1)S(1)} %all_to_all.10), kind=kLoop, calls=%fused_computation.24 | loop fusion | bytes 524288 | tf_op jit(solution)/shard_map/reshape | solution.py:196
  (15 shorter events, 0.2 us)
Async XLA Ops:
  0.0 17.0 %copy-start = (s32[8]{0:T(128)S(1)}, s32[8]{0:T(128)}, u32[]{:S(2)}) copy-start(s32[8]{0:T(128)} %param.9) | copy-start | bytes 100
  6.5 9.6 %copy-start.3 = (s32[8,4]{0,1:T(4,128)S(1)}, s32[8,4]{0,1:T(4,128)}, u32[]{:S(2)}) copy-start(s32[8,4]{0,1:T(4,128)} %param.10) | copy-start | bytes 388
  8.8 33.4 %all-to-all-start = ((bf16[8,130,4,128]{3,2,1,0:T(4,128)(2,1)}), bf16[8,130,4,128]{3,2,1,0:T(4,128)(2,1)S(1)}, u32[]{:S(2)}, u32[]{:S(2)}) async-start(bf16[8,130,4,128]{3,2,1,0:T(4,128)(2,1)} %copy.33), calls=%async_computation | async-start | bytes 2129920 | tf_op jit(solution)/shard_map/all_to_all | solution.py:156
  43.3 1.7 %copy-start.1 = (bf16[1025,32,32]{0,2,1:T(8,128)(2,1)S(1)}, bf16[1025,32,32]{0,2,1:T(8,128)(2,1)}, u32[]{:S(2)}) copy-start(bf16[1025,32,32]{0,2,1:T(8,128)(2,1)} %get-tuple-element.7) | copy-start | bytes 6297604
  43.3 2.4 %copy-start.2 = (bf16[1025,32,32]{0,2,1:T(8,128)(2,1)S(1)}, bf16[1025,32,32]{0,2,1:T(8,128)(2,1)}, u32[]{:S(2)}) copy-start(bf16[1025,32,32]{0,2,1:T(8,128)(2,1)} %get-tuple-element.8) | copy-start | bytes 6297604
where the time goes:
time: 63.3 us; the launch traced here: 62.9 us
  waiting for transfers between devices  18.8 us (30%)
  blocking collectives  12.5 us (20%)
  local copies, waits for them, and re-layouts  11.6 us (18%)
  other arithmetic  8.75 us (14%)
  starting transfers between devices  7.28 us (12%)
  matrix products  3.8 us (6%)
    all_to_all x1, waiting for transfers between devices, local_body(): lax.all_to_all(packed, 'seq', split_axis=0, concat_axis=0, tiled=True)  18.8 us
    all_to_all x1, blocking collectives, local_body(): lax.all_to_all(output.reshape(devices, row_count, own), 'seq', split_axis...  12.5 us
    all_to_all x1, starting transfers between devices, local_body(): lax.all_to_all(packed, 'seq', split_axis=0, concat_axis=0, tiled=True)  7.28 us
    unnamed x12, local copies, waits for them, and re-layouts  4.87 us
    another operation x2, other arithmetic  3.99 us
    transpose x1, local copies, waits for them, and re-layouts, local_body(): packed.reshape(row_count + lib_rows, 4, devices, own).transpose(2, 0, 1, 3)  2.29 us
    dot_general x1, matrix products, local_body(): spec = jnp.dot(table, operands, preferred_element_type=jnp.float32)  2.2 us
    transpose x1, other arithmetic, local_body(): packed.reshape(row_count + lib_rows, 4, devices, own).transpose(2, 0, 1, 3)  1.7 us
  transfers between devices with their start and end apart: 1, of which 1 were waited for; matrix products, arithmetic and copies ran while one was open for 12% of the time, Pallas kernels for 0%

commit v1 on v0

--- a/solution.py
+++ b/solution.py
@@ -153,7 +153,22 @@
     packed = jnp.concatenate([fresh, long_filter.astype(jnp.bfloat16)[:, None, :]], axis=1)
     packed = jnp.concatenate([packed, library.reshape(lib_rows, 4, channels)], axis=0)
     packed = packed.reshape(row_count + lib_rows, 4, devices, own).transpose(2, 0, 1, 3)
-    moved = lax.all_to_all(packed, "seq", split_axis=0, concat_axis=0, tiled=True)
+    odd = lax.axis_size("seq")
+    block_now = lax.axis_index("seq")
+    all_values, w_next = (odd, block_now)
+    y = list(packed.shape)
+    z_new = packed.shape[0] // all_values
+    y[0] = z_new
+    answer = y[0]
+    y[0] = answer * all_values
+    idx = 0
+    moved = jnp.zeros(y, packed.dtype)
+    while idx < all_values:
+        then = lax.dynamic_slice_in_dim(packed, (w_next ^ idx) * z_new, z_new, axis=0)
+        if idx:
+            then = lax.ppermute(then, "seq", [(dd, dd ^ idx) for dd in range(all_values)])
+        moved = lax.dynamic_update_slice_in_dim(moved, then, (w_next ^ idx) * answer, axis=0)
+        idx += 1
     rows = moved[:, :row_count].reshape(tokens, 4, own)
     lib_all = moved[:, row_count:].reshape(devices * lib_here, BLK * own)
     slot_ids = block_slot[prefix_blocks.reshape(-1)]

time: 63.3 us -> 101 us (1.60)
  local copies, waits for them, and re-layouts: 11.6 us -> 61.2 us
  waiting for transfers between devices: 18.8 us -> 0.33 us
  starting transfers between devices: 7.28 us -> 14.6 us
  other arithmetic: 8.75 us -> 7.08 us
    dynamic_update_slice x0 -> x8, local copies, waits for them, and re-layouts: none -> 51 us  [local_body(): lax.dynamic_update_slice_in_dim(moved, then, (w_next ^ idx) * answer, axi...]
    all_to_all x1 -> x0, waiting for transfers between devices: 18.8 us -> none  [local_body(): lax.all_to_all(packed, 'seq', split_axis=0, concat_axis=0, tiled=True)]
    ppermute x0 -> x7, starting transfers between devices: none -> 14.6 us  [local_body(): lax.ppermute(then, 'seq', [(dd, dd ^ idx) for dd in range(all_values)])]
    all_to_all x1 -> x0, starting transfers between devices: 7.28 us -> none  [local_body(): lax.all_to_all(packed, 'seq', split_axis=0, concat_axis=0, tiled=True)]
    ppermute x0 -> x7, local copies, waits for them, and re-layouts: none -> 3.26 us  [local_body(): lax.ppermute(then, 'seq', [(dd, dd ^ idx) for dd in range(all_values)])]
    transpose x1 -> x0, local copies, waits for them, and re-layouts: 2.29 us -> none  [local_body(): packed.reshape(row_count + lib_rows, 4, devices, own).transpose(2, 0, 1, 3)]
    unnamed x12 -> x13, local copies, waits for them, and re-layouts: 4.87 us -> 2.69 us
    transpose x1 -> x0, other arithmetic: 1.7 us -> none  [local_body(): packed.reshape(row_count + lib_rows, 4, devices, own).transpose(2, 0, 1, 3)]
  transfers between devices with their start and end apart: 1 -> 7, of which waited for: 1 -> 1; matrix products, arithmetic and copies ran while one was open for 12% -> 55% of each run, Pallas kernels for 0% -> 0%
where the time goes in v1:
time: 101 us; the launch traced here: 100 us
  local copies, waits for them, and re-layouts  61.2 us (61%)
  starting transfers between devices  14.6 us (14%)
  blocking collectives  12.9 us (13%)
  other arithmetic  7.08 us (7%)
  matrix products  3.79 us (4%)
    dynamic_update_slice x8, local copies, waits for them, and re-layouts, local_body(): lax.dynamic_update_slice_in_dim(moved, then, (w_next ^ idx) * answer, axi...  51 us
    ppermute x7, starting transfers between devices, local_body(): lax.ppermute(then, 'seq', [(dd, dd ^ idx) for dd in range(all_values)])  14.6 us
    all_to_all x1, blocking collectives, local_body(): lax.all_to_all(output.reshape(devices, row_count, own), 'seq', split_axis...  12.9 us
    another operation x2, other arithmetic  3.93 us
    ppermute x7, local copies, waits for them, and re-layouts, local_body(): lax.ppermute(then, 'seq', [(dd, dd ^ idx) for dd in range(all_values)])  3.26 us
    unnamed x13, local copies, waits for them, and re-layouts  2.69 us
    dot_general x1, matrix products, local_body(): spec = jnp.dot(table, operands, preferred_element_type=jnp.float32)  2.19 us
  transfers between devices with their start and end apart: 7, of which 1 were waited for; matrix products, arithmetic and copies ran while one was open for 55% of the time, Pallas kernels for 0%

profile of v1, /device:TPU:0, one launch (start us, length us, event | category | flops | bytes accessed | tf_op | source)
XLA Modules:
  0.0 100.4 jit_solution(4167126773007965421)
XLA Ops:
  0.0 0.8 copy.28
  0.8 1.1 %convert_bitcast_fusion = bf16[16,8,8,128]{3,1,2,0:T(8,128)(2,1)S(1)} fusion(f32[128,1024]{1,0:T(8,128)} %param.12), kind=kLoop, calls=%fused_computation.28 | loop fusion | flops 131072 | bytes 786432
  2.5 6.1 %collective-permute-start.6 = (bf16[1,130,4,128]{3,1,2,0:T(8,128)(2,1)S(1)}, bf16[1,130,4,128]{3,1,2,0:T(8,128)(2,1)S(1)}, u32[]{:S(2)}, u32[]{:S(2)}) collective-permute-start(bf16[1,130,4,128]{3,1,2,0:T(8,128)(2,1)S(1)} %get-tuple-element.7), channel_id=1, source_target_pairs={{0,14},{2,12},{4,10},{6,8},{8,6},{10,4},{12,2},{14,0},{1,15},{3,13... | collective-permute-start | bytes 399368 | tf_op jit(solution)/shard_map/ppermute | solution.py:169
  8.8 0.8 collective-permute-start.4
  9.5 3.4 %collective-permute-start.1 = (bf16[1,130,4,128]{3,1,2,0:T(8,128)(2,1)S(1)}, bf16[1,130,4,128]{3,1,2,0:T(8,128)(2,1)S(1)}, u32[]{:S(2)}, u32[]{:S(2)}) collective-permute-start(bf16[1,130,4,128]{3,1,2,0:T(8,128)(2,1)S(1)} %get-tuple-element.12), channel_id=1, source_target_pairs={{0,4},{2,6},{4,0},{6,2},{8,12},{10,14},{12,8},{14,10},{1,5},{3,7},... | collective-permute-start | bytes 399368 | tf_op jit(solution)/shard_map/ppermute | solution.py:169
  12.9 1.5 %collective-permute-start = (bf16[1,130,4,128]{3,1,2,0:T(8,128)(2,1)S(1)}, bf16[1,130,4,128]{3,1,2,0:T(8,128)(2,1)S(1)}, u32[]{:S(2)}, u32[]{:S(2)}) collective-permute-start(bf16[1,130,4,128]{3,1,2,0:T(8,128)(2,1)S(1)} %get-tuple-element.13), channel_id=1, source_target_pairs={{0,2},{2,0},{4,6},{6,4},{8,10},{10,8},{12,14},{14,12},{1,3},{3,1},... | collective-permute-start | bytes 399368 | tf_op jit(solution)/shard_map/ppermute | solution.py:169
  14.4 0.6 fusion.25
  15.2 0.7 fusion.28
  15.8 3.6 %subtract_convert_fusion = (bf16[1025,32,32]{0,2,1:T(8,128)(2,1)}, bf16[1025,32,32]{0,2,1:T(8,128)(2,1)}) fusion(f32[1025,32]{0,1:T(8,128)S(1)} %get-tuple-element.22, f32[1025,32]{0,1:T(8,128)S(1)} %get-tuple-element.21, f32[1025,32]{0,1:T(8,128)S(1)} %get-tuple-element.23, f32[1025,32]{0,1:T(8,128)S(1)} %get-tuple-element.20), kind=kLoop, calls=%fused_computation.2 | loop fusion | flops 8396800 | bytes 4723200 | tf_op jit(solution)/shard_map/convert.5
  19.5 0.7 fusion.32
  20.5 1.5 %collective-permute-start.3 = (bf16[1,130,4,128]{3,1,2,0:T(8,128)(2,1)S(1)}, bf16[1,130,4,128]{3,1,2,0:T(8,128)(2,1)}, u32[]{:S(2)}, u32[]{:S(2)}) collective-permute-start(bf16[1,130,4,128]{3,1,2,0:T(8,128)(2,1)S(1)} %get-tuple-element.10), channel_id=1, source_target_pairs={{0,8},{2,10},{4,12},{6,14},{8,0},{10,2},{12,4},{14,6},{1,9},{3,11}... | collective-permute-start | bytes 399368 | tf_op jit(solution)/shard_map/ppermute | solution.py:169
  22.0 1.2 %collective-permute-start.2 = (bf16[1,130,4,128]{3,1,2,0:T(8,128)(2,1)S(1)}, bf16[1,130,4,128]{3,1,2,0:T(8,128)(2,1)}, u32[]{:S(2)}, u32[]{:S(2)}) collective-permute-start(bf16[1,130,4,128]{3,1,2,0:T(8,128)(2,1)S(1)} %get-tuple-element.11), channel_id=1, source_target_pairs={{0,6},{2,4},{4,2},{6,0},{8,14},{10,12},{12,10},{14,8},{1,7},{3,5},... | collective-permute-start | bytes 399368 | tf_op jit(solution)/shard_map/ppermute | solution.py:169
  23.3 0.8 dynamic_slice.39
  24.2 0.7 gather_fusion
  25.1 6.5 %dynamic_update_slice.24 = bf16[8,130,4,128]{3,0,2,1:T(8,128)(2,1)S(1)} dynamic-update-slice(bf16[8,130,4,128]{3,0,2,1:T(8,128)(2,1)S(1)} %broadcast_in_dim.10, bf16[1,130,4,128]{3,0,2,1:T(2,128)(2,1)S(1)} %copy.14, s32[]{:T(128)S(6)} %select_n.86, s32[]{:T(128)} %constant.22.clone.1, s32[]{:T(128)} %constant.22.clone.1, s32[]{:T(128)} %constant.22.clone.1) | dynamic-update-slice | bytes 266244 | tf_op jit(solution)/shard_map/dynamic_update_slice | solution.py:170
  31.9 6.4 %dynamic_update_slice.25 = bf16[8,130,4,128]{3,0,2,1:T(8,128)(2,1)S(1)} dynamic-update-slice(bf16[8,130,4,128]{3,0,2,1:T(8,128)(2,1)S(1)} %dynamic_update_slice.24, bf16[1,130,4,128]{3,0,2,1:T(2,128)(2,1)S(1)} %copy.15, s32[]{:T(128)S(6)} %select_n.87, s32[]{:T(128)} %constant.22.clone.1, s32[]{:T(128)} %constant.22.clone.1, s32[]{:T(128)} %constant.22.clone.1) | dynamic-update-slice | bytes 266244 | tf_op jit(solution)/shard_map/dynamic_update_slice | solution.py:170
  38.4 6.4 %dynamic_update_slice.26 = bf16[8,130,4,128]{3,0,2,1:T(8,128)(2,1)S(1)} dynamic-update-slice(bf16[8,130,4,128]{3,0,2,1:T(8,128)(2,1)S(1)} %dynamic_update_slice.25, bf16[1,130,4,128]{3,0,2,1:T(2,128)(2,1)S(1)} %copy.16, s32[]{:T(128)S(6)} %select_n.88, s32[]{:T(128)} %constant.22.clone.1, s32[]{:T(128)} %constant.22.clone.1, s32[]{:T(128)} %constant.22.clone.1) | dynamic-update-slice | bytes 266244 | tf_op jit(solution)/shard_map/dynamic_update_slice | solution.py:170
  44.8 1.1 %copy.17 = bf16[1,130,4,128]{3,0,2,1:T(2,128)(2,1)S(1)} copy(bf16[1,130,4,128]{3,1,2,0:T(8,128)(2,1)} %collective-permute-done.2) | data formatting | bytes 266240 | tf_op jit(solution)/shard_map/ppermute | solution.py:169
  45.9 6.4 %dynamic_update_slice.27 = bf16[8,130,4,128]{3,0,2,1:T(8,128)(2,1)S(1)} dynamic-update-slice(bf16[8,130,4,128]{3,0,2,1:T(8,128)(2,1)S(1)} %dynamic_update_slice.26, bf16[1,130,4,128]{3,0,2,1:T(2,128)(2,1)S(1)} %copy.17, s32[]{:T(128)S(6)} %select_n.89, s32[]{:T(128)} %constant.22.clone.1, s32[]{:T(128)} %constant.22.clone.1, s32[]{:T(128)} %constant.22.clone.1) | dynamic-update-slice | bytes 266244 | tf_op jit(solution)/shard_map/dynamic_update_slice | solution.py:170
  52.3 1.1 %copy.18 = bf16[1,130,4,128]{3,0,2,1:T(2,128)(2,1)S(1)} copy(bf16[1,130,4,128]{3,1,2,0:T(8,128)(2,1)} %collective-permute-done.3) | data formatting | bytes 266240 | tf_op jit(solution)/shard_map/ppermute | solution.py:169
  53.4 6.4 %dynamic_update_slice.28 = bf16[8,130,4,128]{3,0,2,1:T(8,128)(2,1)S(1)} dynamic-update-slice(bf16[8,130,4,128]{3,0,2,1:T(8,128)(2,1)S(1)} %dynamic_update_slice.27, bf16[1,130,4,128]{3,0,2,1:T(2,128)(2,1)S(1)} %copy.18, s32[]{:T(128)S(6)} %select_n.90, s32[]{:T(128)} %constant.22.clone.1, s32[]{:T(128)} %constant.22.clone.1, s32[]{:T(128)} %constant.22.clone.1) | dynamic-update-slice | bytes 266244 | tf_op jit(solution)/shard_map/dynamic_update_slice | solution.py:170
  60.0 6.4 %dynamic_update_slice.29 = bf16[8,130,4,128]{3,0,2,1:T(8,128)(2,1)S(1)} dynamic-update-slice(bf16[8,130,4,128]{3,0,2,1:T(8,128)(2,1)S(1)} %dynamic_update_slice.28, bf16[1,130,4,128]{3,0,2,1:T(2,128)(2,1)S(1)} %copy.19, s32[]{:T(128)S(6)} %select_n.91, s32[]{:T(128)} %constant.22.clone.1, s32[]{:T(128)} %constant.22.clone.1, s32[]{:T(128)} %constant.22.clone.1) | dynamic-update-slice | bytes 266244 | tf_op jit(solution)/shard_map/dynamic_update_slice | solution.py:170
  66.6 6.4 %dynamic_update_slice.30 = bf16[8,130,4,128]{3,0,2,1:T(8,128)(2,1)S(1)} dynamic-update-slice(bf16[8,130,4,128]{3,0,2,1:T(8,128)(2,1)S(1)} %dynamic_update_slice.29, bf16[1,130,4,128]{3,0,2,1:T(2,128)(2,1)S(1)} %copy.20, s32[]{:T(128)S(6)} %select_n.92, s32[]{:T(128)} %constant.22.clone.1, s32[]{:T(128)} %constant.22.clone.1, s32[]{:T(128)} %constant.22.clone.1) | dynamic-update-slice | bytes 266244 | tf_op jit(solution)/shard_map/dynamic_update_slice | solution.py:170
  73.2 6.4 %dynamic_update_slice.31 = bf16[8,130,4,128]{3,0,2,1:T(8,128)(2,1)S(1)} dynamic-update-slice(bf16[8,130,4,128]{3,0,2,1:T(8,128)(2,1)S(1)} %dynamic_update_slice.30, bf16[1,130,4,128]{3,0,2,1:T(2,128)(2,1)S(1)} %copy.21, s32[]{:T(128)S(6)} %select_n.93, s32[]{:T(128)} %constant.22.clone.1, s32[]{:T(128)} %constant.22.clone.1, s32[]{:T(128)} %constant.22.clone.1) | dynamic-update-slice | bytes 266244 | tf_op jit(solution)/shard_map/dynamic_update_slice | solution.py:170
  79.6 0.4 copy.22
  80.5 0.5 multiply_add_fusion
  81.1 1.0 %copy-done.2 = bf16[1025,32,32]{0,2,1:T(8,128)(2,1)S(1)} copy-done((bf16[1025,32,32]{0,2,1:T(8,128)(2,1)S(1)}, bf16[1025,32,32]{0,2,1:T(8,128)(2,1)}, u32[]{:S(2)}) %copy-start.2) | copy-done | bytes 2099224
  82.2 0.7 copy-done.3
  82.9 2.2 %fusion.1 = f32[2050,256]{1,0:T(8,128)S(1)} fusion(bf16[1025,1024]{0,1:T(8,128)(2,1)S(1)} %bitcast.75, bf16[1025,1024]{0,1:T(8,128)(2,1)S(1)} %bitcast.73, bf16[1024,128]{1,0:T(8,128)(2,1)S(1)} %slice_bitcast_fusion.1, bf16[1024,128]{1,0:T(8,128)(2,1)S(1)} %fusion.12), kind=kOutput, calls=%fused_computation.5 | convolution fusion | flops 1084235776 | bytes 6821888 | tf_op jit(solution)/shard_map/dot_general | solution.py:194
  85.4 1.4 %fusion.4 = bf16[1024,128]{1,0:T(8,128)(2,1)S(1)} fusion(bf16[1025,1024]{0,1:T(8,128)(2,1)S(1)} %bitcast.76, bf16[1025,1024]{0,1:T(8,128)(2,1)S(1)} %bitcast.74, bf16[1025,128]{1,0:T(8,128)(2,1)S(1)} %get-tuple-element.6, bf16[1025,128]{1,0:T(8,128)(2,1)S(1)} %get-tuple-element.5, f32[1024,3,128]{2,0,1:T(8,128)S(1)} %multiply_add_fusion, ...), kind=kOutput, calls=%fused_computation.9 | convolution fusion | flops 547496960 | bytes 6558720 | tf_op jit(solution)/shard_map/dot_general | solution.py:204
  86.8 12.9 %all_to_all.5 = bf16[8,128,128]{2,1,0:T(8,128)(2,1)S(1)} all-to-all(bf16[8,128,128]{2,1,0:T(8,128)(2,1)S(1)} %bitcast.78), channel_id=1, replica_groups=mesh['group'=2,'seq'=8,'chan'=2] {'seq'}, dimensions={0} | all-to-all | bytes 524288 | tf_op jit(solution)/shard_map/all_to_all | solution.py:208
  99.6 0.7 copy_bitcast_fusion.1
  (46 shorter events, 3.5 us)
Async XLA Ops:
  0.0 2.0 %copy-start = (bf16[128,3,1024]{2,0,1:T(8,128)(2,1)S(1)}, bf16[128,3,1024]{2,0,1:T(8,128)(2,1)}, u32[]{:S(2)}) copy-start(bf16[128,3,1024]{2,0,1:T(8,128)(2,1)} %param.7) | copy-start | bytes 2359300
  2.3 12.7 %copy-start.4 = (s32[8,4]{0,1:T(4,128)S(1)}, s32[8,4]{0,1:T(4,128)}, u32[]{:S(2)}) copy-start(s32[8,4]{0,1:T(4,128)} %param.10) | copy-start | bytes 388
  2.5 70.5 %collective-permute-start.6 = (bf16[1,130,4,128]{3,1,2,0:T(8,128)(2,1)S(1)}, bf16[1,130,4,128]{3,1,2,0:T(8,128)(2,1)S(1)}, u32[]{:S(2)}, u32[]{:S(2)}) collective-permute-start(bf16[1,130,4,128]{3,1,2,0:T(8,128)(2,1)S(1)} %get-tuple-element.7), channel_id=1, source_target_pairs={{0,14},{2,12},{4,10},{6,8},{8,6},{10,4},{12,2},{14,0},{1,15},{3,13... | collective-permute-start | bytes 399368 | tf_op jit(solution)/shard_map/ppermute | solution.py:169
  8.6 57.8 %collective-permute-start.5 = (bf16[1,130,4,128]{3,1,2,0:T(8,128)(2,1)S(1)}, bf16[1,130,4,128]{3,1,2,0:T(8,128)(2,1)S(1)}, u32[]{:S(2)}, u32[]{:S(2)}) collective-permute-start(bf16[1,130,4,128]{3,1,2,0:T(8,128)(2,1)S(1)} %get-tuple-element.8), channel_id=1, source_target_pairs={{0,12},{2,14},{4,8},{6,10},{8,4},{10,6},{12,0},{14,2},{1,13},{3,15... | collective-permute-start | bytes 399368 | tf_op jit(solution)/shard_map/ppermute | solution.py:169
  8.8 51.0 %collective-permute-start.4 = (bf16[1,130,4,128]{3,1,2,0:T(8,128)(2,1)S(1)}, bf16[1,130,4,128]{3,1,2,0:T(8,128)(2,1)S(1)}, u32[]{:S(2)}, u32[]{:S(2)}) collective-permute-start(bf16[1,130,4,128]{3,1,2,0:T(8,128)(2,1)S(1)} %get-tuple-element.9), channel_id=1, source_target_pairs={{0,10},{2,8},{4,14},{6,12},{8,2},{10,0},{12,6},{14,4},{1,11},{3,9}... | collective-permute-start | bytes 399368 | tf_op jit(solution)/shard_map/ppermute | solution.py:169
  9.5 11.0 %collective-permute-start.1 = (bf16[1,130,4,128]{3,1,2,0:T(8,128)(2,1)S(1)}, bf16[1,130,4,128]{3,1,2,0:T(8,128)(2,1)S(1)}, u32[]{:S(2)}, u32[]{:S(2)}) collective-permute-start(bf16[1,130,4,128]{3,1,2,0:T(8,128)(2,1)S(1)} %get-tuple-element.12), channel_id=1, source_target_pairs={{0,4},{2,6},{4,0},{6,2},{8,12},{10,14},{12,8},{14,10},{1,5},{3,7},... | collective-permute-start | bytes 399368 | tf_op jit(solution)/shard_map/ppermute | solution.py:169
  12.9 9.1 %collective-permute-start = (bf16[1,130,4,128]{3,1,2,0:T(8,128)(2,1)S(1)}, bf16[1,130,4,128]{3,1,2,0:T(8,128)(2,1)S(1)}, u32[]{:S(2)}, u32[]{:S(2)}) collective-permute-start(bf16[1,130,4,128]{3,1,2,0:T(8,128)(2,1)S(1)} %get-tuple-element.13), channel_id=1, source_target_pairs={{0,2},{2,0},{4,6},{6,4},{8,10},{10,8},{12,14},{14,12},{1,3},{3,1},... | collective-permute-start | bytes 399368 | tf_op jit(solution)/shard_map/ppermute | solution.py:169
  15.8 8.4 %copy-start.1 = (s32[8]{0:T(128)S(1)}, s32[8]{0:T(128)}, u32[]{:S(2)}) copy-start(s32[8]{0:T(128)} %param.9) | copy-start | bytes 100
  20.5 31.8 %collective-permute-start.3 = (bf16[1,130,4,128]{3,1,2,0:T(8,128)(2,1)S(1)}, bf16[1,130,4,128]{3,1,2,0:T(8,128)(2,1)}, u32[]{:S(2)}, u32[]{:S(2)}) collective-permute-start(bf16[1,130,4,128]{3,1,2,0:T(8,128)(2,1)S(1)} %get-tuple-element.10), channel_id=1, source_target_pairs={{0,8},{2,10},{4,12},{6,14},{8,0},{10,2},{12,4},{14,6},{1,9},{3,11}... | collective-permute-start | bytes 399368 | tf_op jit(solution)/shard_map/ppermute | solution.py:169
  22.0 22.8 %collective-permute-start.2 = (bf16[1,130,4,128]{3,1,2,0:T(8,128)(2,1)S(1)}, bf16[1,130,4,128]{3,1,2,0:T(8,128)(2,1)}, u32[]{:S(2)}, u32[]{:S(2)}) collective-permute-start(bf16[1,130,4,128]{3,1,2,0:T(8,128)(2,1)S(1)} %get-tuple-element.11), channel_id=1, source_target_pairs={{0,6},{2,4},{4,2},{6,0},{8,14},{10,12},{12,10},{14,8},{1,7},{3,5},... | collective-permute-start | bytes 399368 | tf_op jit(solution)/shard_map/ppermute | solution.py:169
  80.5 1.7 %copy-start.2 = (bf16[1025,32,32]{0,2,1:T(8,128)(2,1)S(1)}, bf16[1025,32,32]{0,2,1:T(8,128)(2,1)}, u32[]{:S(2)}) copy-start(bf16[1025,32,32]{0,2,1:T(8,128)(2,1)} %get-tuple-element.15) | copy-start | bytes 6297604
  80.5 2.4 %copy-start.3 = (bf16[1025,32,32]{0,2,1:T(8,128)(2,1)S(1)}, bf16[1025,32,32]{0,2,1:T(8,128)(2,1)}, u32[]{:S(2)}) copy-start(bf16[1025,32,32]{0,2,1:T(8,128)(2,1)} %get-tuple-element.16) | copy-start | bytes 6297604
